TPU v7x, 256 devices: a whole 4x4x8 slice. The times are simulated.
256 devices in a mesh: ctx: 32 (over z, x), tp: 8 (over y, core).
Axes of the slice: x: 4, y: 4, z: 8, core: 2. Of those that a mesh axis runs over, the one named last changes fastest.
Arguments:
- tokens: bfloat16 [16384, 3072], P(('ctx', 'tp')), may hold values from -6 to 6
- w_query: bfloat16 [3072, 4096], P(None, 'tp'), may hold values from -0.109375 to 0.109375
- w_key: bfloat16 [3072, 4096], P(None, 'tp'), may hold values from -0.109375 to 0.109375
- w_value: bfloat16 [3072, 4096], P(None, 'tp'), may hold values from -0.109375 to 0.109375
- norm_gain: float32 [4096], P('tp'), may hold values from 0.1 to 1.9
Outputs:
- attended: bfloat16 [16384, 4096], P('ctx', 'tp')
All inputs are finite; a program needn't handle non-finite values.
Results may differ from a plain program's by a relative error of at most 0.0062.
Values may be sent and summed in bfloat16 or wider, within the bound.
No kernel may reach another device: no remote copies, remote signals or barrier semaphores. Data moves between devices by JAX's collectives and lax.ppermute only.
A program may use at most 64 MiB of HBM per device.

v0:
```python
import jax
import jax.numpy as jnp
from jax import lax
from jax.sharding import PartitionSpec as P

HEAD_DIM = 128
BLOCK = 512
EPSILON = 1e-06


def from_behind(value, axis, by):
    size = lax.axis_size(axis)
    pairs = [(i, i + by) for i in range(size) if 0 <= i + by < size]
    return lax.ppermute(value, axis, pairs)


def body(tokens, w_query, w_key, w_value, norm_gain):
    local_width = w_query.shape[1]
    head_count = local_width // HEAD_DIM
    piece_rows = lax.all_gather(tokens, "tp", axis=0, tiled=True)
    query_part = jnp.dot(piece_rows, w_query, preferred_element_type=jnp.float32).astype(
        jnp.bfloat16
    )
    key_part = jnp.dot(piece_rows, w_key, preferred_element_type=jnp.float32).astype(jnp.bfloat16)
    value_part = jnp.dot(piece_rows, w_value, preferred_element_type=jnp.float32).astype(
        jnp.bfloat16
    )
    projected = jnp.concatenate([query_part, key_part, value_part], axis=1)
    group_len = projected.shape[0]
    block_count = group_len // BLOCK
    shaped = projected.reshape(block_count, BLOCK, 3, head_count, HEAD_DIM)
    query_rows = shaped[:, :, 0]
    key_rows = shaped[:, :, 1]
    value_rows = shaped[:, :, 2]
    block_states = jnp.einsum(
        "bshd,bshe->bhde", key_rows, value_rows, preferred_element_type=jnp.float32
    )
    local_state = jnp.sum(block_states, axis=0)
    empty_state = jnp.zeros_like(local_state)

    def advance(step_index, carried):
        return from_behind(carried + local_state, "ctx", 1)

    prefix_state = lax.fori_loop(0, lax.axis_size("ctx") - 1, advance, empty_state)
    running = jnp.cumsum(block_states, axis=0)
    earlier = jnp.concatenate([jnp.zeros_like(block_states), running[:-1]], axis=0)
    block_start = prefix_state[None] + earlier
    scores = jnp.einsum("bqhd,bkhd->bhqk", query_rows, key_rows, preferred_element_type=jnp.float32)
    causal = jnp.arange(BLOCK)[:, None] >= jnp.arange(BLOCK)[None, :]
    scores = jnp.where(causal[None, None], scores, jnp.float32(0.0)).astype(jnp.bfloat16)
    inner = jnp.einsum("bhqk,bkhe->bqhe", scores, value_rows, preferred_element_type=jnp.float32)
    carried_part = jnp.einsum(
        "bqhd,bhde->bqhe",
        query_rows.astype(jnp.float32),
        block_start,
        precision=lax.Precision.HIGHEST,
    )
    mixed = inner + carried_part
    mean_square = jnp.mean(mixed * mixed, axis=-1, keepdims=True)
    normed = mixed * lax.rsqrt(mean_square + EPSILON) * norm_gain.reshape(head_count, HEAD_DIM)
    return normed.reshape(group_len, local_width).astype(jnp.bfloat16)


def solution(mesh):
    placed = (P(("ctx", "tp"), None), P(None, "tp"), P(None, "tp"), P(None, "tp"), P("tp"))
    return jax.shard_map(
        body, mesh=mesh, in_specs=placed, out_specs=P("ctx", "tp"), check_vma=False
    )
```

profile of v0, /device:TPU:128, one launch (start us, length us, event | category | flops | bytes accessed | tf_op | source)
XLA Modules:
  0.0 505.0 jit_solution(23542777974359117)
XLA Ops:
  8.0 32.9 %all-gather.2.cloned.1.call-done = bf16[512,3072]{1,0:T(8,128)(2,1)} async-done(((bf16[64,3072]{1,0:T(8,128)(2,1)}), bf16[512,3072]{1,0:T(8,128)(2,1)}) %all-gather.2.cloned.1.call-update) | async-done | bytes 3145744 | tf_op jit(solution)/shard_map/all_gather | solution.py:20
  41.0 3.9 convolution_convert_fusion
  50.9 436.2 %while.10 = (s32[]{:T(128)}, f32[4,128,128]{2,1,0:T(8,128)S(1)}, f32[4,128,128]{2,1,0:T(8,128)}, s32[]{:T(128)}) while((s32[]{:T(128)}, f32[4,128,128]{2,1,0:T(8,128)S(1)}, f32[4,128,128]{2,1,0:T(8,128)}, s32[]{:T(128)}) %tuple.19), condition=%wide.region_1.0_spmd, body=%wide.region_0.0_spmd.sunk | while | flops 65538 | bytes 1835101 | solution.py:44
  52.6 3.4 collective-permute-start
  56.0 10.5 %collective-permute-done = f32[4,128,128]{2,1,0:T(8,128)S(1)} collective-permute-done((f32[4,128,128]{2,1,0:T(8,128)}, f32[4,128,128]{2,1,0:T(8,128)S(1)}, u32[]{:S(2)}, u32[]{:S(2)}) %collective-permute-start) | collective-permute-done | bytes 262176 | tf_op jit(solution)/shard_map/while/body/eval_jaxpr/ppermute | solution.py:14
  68.1 1.9 collective-permute-start
  70.0 11.1 %collective-permute-done = f32[4,128,128]{2,1,0:T(8,128)S(1)} collective-permute-done((f32[4,128,128]{2,1,0:T(8,128)}, f32[4,128,128]{2,1,0:T(8,128)S(1)}, u32[]{:S(2)}, u32[]{:S(2)}) %collective-permute-start) | collective-permute-done | bytes 262176 | tf_op jit(solution)/shard_map/while/body/eval_jaxpr/ppermute | solution.py:14
  82.8 1.9 collective-permute-start
  84.7 10.2 %collective-permute-done = f32[4,128,128]{2,1,0:T(8,128)S(1)} collective-permute-done((f32[4,128,128]{2,1,0:T(8,128)}, f32[4,128,128]{2,1,0:T(8,128)S(1)}, u32[]{:S(2)}, u32[]{:S(2)}) %collective-permute-start) | collective-permute-done | bytes 262176 | tf_op jit(solution)/shard_map/while/body/eval_jaxpr/ppermute | solution.py:14
  96.6 1.9 collective-permute-start
  98.5 9.9 %collective-permute-done = f32[4,128,128]{2,1,0:T(8,128)S(1)} collective-permute-done((f32[4,128,128]{2,1,0:T(8,128)}, f32[4,128,128]{2,1,0:T(8,128)S(1)}, u32[]{:S(2)}, u32[]{:S(2)}) %collective-permute-start) | collective-permute-done | bytes 262176 | tf_op jit(solution)/shard_map/while/body/eval_jaxpr/ppermute | solution.py:14
  110.1 1.9 collective-permute-start
  112.0 9.9 %collective-permute-done = f32[4,128,128]{2,1,0:T(8,128)S(1)} collective-permute-done((f32[4,128,128]{2,1,0:T(8,128)}, f32[4,128,128]{2,1,0:T(8,128)S(1)}, u32[]{:S(2)}, u32[]{:S(2)}) %collective-permute-start) | collective-permute-done | bytes 262176 | tf_op jit(solution)/shard_map/while/body/eval_jaxpr/ppermute | solution.py:14
  123.5 1.9 collective-permute-start
  125.4 9.9 %collective-permute-done = f32[4,128,128]{2,1,0:T(8,128)S(1)} collective-permute-done((f32[4,128,128]{2,1,0:T(8,128)}, f32[4,128,128]{2,1,0:T(8,128)S(1)}, u32[]{:S(2)}, u32[]{:S(2)}) %collective-permute-start) | collective-permute-done | bytes 262176 | tf_op jit(solution)/shard_map/while/body/eval_jaxpr/ppermute | solution.py:14
  137.0 1.9 collective-permute-start
  138.9 9.9 %collective-permute-done = f32[4,128,128]{2,1,0:T(8,128)S(1)} collective-permute-done((f32[4,128,128]{2,1,0:T(8,128)}, f32[4,128,128]{2,1,0:T(8,128)S(1)}, u32[]{:S(2)}, u32[]{:S(2)}) %collective-permute-start) | collective-permute-done | bytes 262176 | tf_op jit(solution)/shard_map/while/body/eval_jaxpr/ppermute | solution.py:14
  150.4 1.9 collective-permute-start
  152.3 9.9 %collective-permute-done = f32[4,128,128]{2,1,0:T(8,128)S(1)} collective-permute-done((f32[4,128,128]{2,1,0:T(8,128)}, f32[4,128,128]{2,1,0:T(8,128)S(1)}, u32[]{:S(2)}, u32[]{:S(2)}) %collective-permute-start) | collective-permute-done | bytes 262176 | tf_op jit(solution)/shard_map/while/body/eval_jaxpr/ppermute | solution.py:14
  163.9 1.9 collective-permute-start
  165.8 9.9 %collective-permute-done = f32[4,128,128]{2,1,0:T(8,128)S(1)} collective-permute-done((f32[4,128,128]{2,1,0:T(8,128)}, f32[4,128,128]{2,1,0:T(8,128)S(1)}, u32[]{:S(2)}, u32[]{:S(2)}) %collective-permute-start) | collective-permute-done | bytes 262176 | tf_op jit(solution)/shard_map/while/body/eval_jaxpr/ppermute | solution.py:14
  179.3 10.6 %collective-permute-done = f32[4,128,128]{2,1,0:T(8,128)S(1)} collective-permute-done((f32[4,128,128]{2,1,0:T(8,128)}, f32[4,128,128]{2,1,0:T(8,128)S(1)}, u32[]{:S(2)}, u32[]{:S(2)}) %collective-permute-start) | collective-permute-done | bytes 262176 | tf_op jit(solution)/shard_map/while/body/eval_jaxpr/ppermute | solution.py:14
  191.5 1.9 collective-permute-start
  193.4 11.7 %collective-permute-done = f32[4,128,128]{2,1,0:T(8,128)S(1)} collective-permute-done((f32[4,128,128]{2,1,0:T(8,128)}, f32[4,128,128]{2,1,0:T(8,128)S(1)}, u32[]{:S(2)}, u32[]{:S(2)}) %collective-permute-start) | collective-permute-done | bytes 262176 | tf_op jit(solution)/shard_map/while/body/eval_jaxpr/ppermute | solution.py:14
  206.8 1.9 collective-permute-start
  208.7 12.5 %collective-permute-done = f32[4,128,128]{2,1,0:T(8,128)S(1)} collective-permute-done((f32[4,128,128]{2,1,0:T(8,128)}, f32[4,128,128]{2,1,0:T(8,128)S(1)}, u32[]{:S(2)}, u32[]{:S(2)}) %collective-permute-start) | collective-permute-done | bytes 262176 | tf_op jit(solution)/shard_map/while/body/eval_jaxpr/ppermute | solution.py:14
  222.9 1.9 collective-permute-start
  224.8 11.6 %collective-permute-done = f32[4,128,128]{2,1,0:T(8,128)S(1)} collective-permute-done((f32[4,128,128]{2,1,0:T(8,128)}, f32[4,128,128]{2,1,0:T(8,128)S(1)}, u32[]{:S(2)}, u32[]{:S(2)}) %collective-permute-start) | collective-permute-done | bytes 262176 | tf_op jit(solution)/shard_map/while/body/eval_jaxpr/ppermute | solution.py:14
  238.1 1.9 collective-permute-start
  240.0 10.8 %collective-permute-done = f32[4,128,128]{2,1,0:T(8,128)S(1)} collective-permute-done((f32[4,128,128]{2,1,0:T(8,128)}, f32[4,128,128]{2,1,0:T(8,128)S(1)}, u32[]{:S(2)}, u32[]{:S(2)}) %collective-permute-start) | collective-permute-done | bytes 262176 | tf_op jit(solution)/shard_map/while/body/eval_jaxpr/ppermute | solution.py:14
  254.4 9.9 %collective-permute-done = f32[4,128,128]{2,1,0:T(8,128)S(1)} collective-permute-done((f32[4,128,128]{2,1,0:T(8,128)}, f32[4,128,128]{2,1,0:T(8,128)S(1)}, u32[]{:S(2)}, u32[]{:S(2)}) %collective-permute-start) | collective-permute-done | bytes 262176 | tf_op jit(solution)/shard_map/while/body/eval_jaxpr/ppermute | solution.py:14
  266.0 1.9 collective-permute-start
  267.9 9.9 %collective-permute-done = f32[4,128,128]{2,1,0:T(8,128)S(1)} collective-permute-done((f32[4,128,128]{2,1,0:T(8,128)}, f32[4,128,128]{2,1,0:T(8,128)S(1)}, u32[]{:S(2)}, u32[]{:S(2)}) %collective-permute-start) | collective-permute-done | bytes 262176 | tf_op jit(solution)/shard_map/while/body/eval_jaxpr/ppermute | solution.py:14
  281.3 9.9 %collective-permute-done = f32[4,128,128]{2,1,0:T(8,128)S(1)} collective-permute-done((f32[4,128,128]{2,1,0:T(8,128)}, f32[4,128,128]{2,1,0:T(8,128)S(1)}, u32[]{:S(2)}, u32[]{:S(2)}) %collective-permute-start) | collective-permute-done | bytes 262176 | tf_op jit(solution)/shard_map/while/body/eval_jaxpr/ppermute | solution.py:14
  292.9 1.9 collective-permute-start
  294.8 9.9 %collective-permute-done = f32[4,128,128]{2,1,0:T(8,128)S(1)} collective-permute-done((f32[4,128,128]{2,1,0:T(8,128)}, f32[4,128,128]{2,1,0:T(8,128)S(1)}, u32[]{:S(2)}, u32[]{:S(2)}) %collective-permute-start) | collective-permute-done | bytes 262176 | tf_op jit(solution)/shard_map/while/body/eval_jaxpr/ppermute | solution.py:14
  306.3 1.9 collective-permute-start
  308.3 9.9 %collective-permute-done = f32[4,128,128]{2,1,0:T(8,128)S(1)} collective-permute-done((f32[4,128,128]{2,1,0:T(8,128)}, f32[4,128,128]{2,1,0:T(8,128)S(1)}, u32[]{:S(2)}, u32[]{:S(2)}) %collective-permute-start) | collective-permute-done | bytes 262176 | tf_op jit(solution)/shard_map/while/body/eval_jaxpr/ppermute | solution.py:14
  319.8 1.9 collective-permute-start
  321.7 9.9 %collective-permute-done = f32[4,128,128]{2,1,0:T(8,128)S(1)} collective-permute-done((f32[4,128,128]{2,1,0:T(8,128)}, f32[4,128,128]{2,1,0:T(8,128)S(1)}, u32[]{:S(2)}, u32[]{:S(2)}) %collective-permute-start) | collective-permute-done | bytes 262176 | tf_op jit(solution)/shard_map/while/body/eval_jaxpr/ppermute | solution.py:14
  333.2 1.9 collective-permute-start
  335.2 9.9 %collective-permute-done = f32[4,128,128]{2,1,0:T(8,128)S(1)} collective-permute-done((f32[4,128,128]{2,1,0:T(8,128)}, f32[4,128,128]{2,1,0:T(8,128)S(1)}, u32[]{:S(2)}, u32[]{:S(2)}) %collective-permute-start) | collective-permute-done | bytes 262176 | tf_op jit(solution)/shard_map/while/body/eval_jaxpr/ppermute | solution.py:14
  346.7 1.9 collective-permute-start
  348.6 10.9 %collective-permute-done = f32[4,128,128]{2,1,0:T(8,128)S(1)} collective-permute-done((f32[4,128,128]{2,1,0:T(8,128)}, f32[4,128,128]{2,1,0:T(8,128)S(1)}, u32[]{:S(2)}, u32[]{:S(2)}) %collective-permute-start) | collective-permute-done | bytes 262176 | tf_op jit(solution)/shard_map/while/body/eval_jaxpr/ppermute | solution.py:14
  361.2 1.9 collective-permute-start
  363.1 12.0 %collective-permute-done = f32[4,128,128]{2,1,0:T(8,128)S(1)} collective-permute-done((f32[4,128,128]{2,1,0:T(8,128)}, f32[4,128,128]{2,1,0:T(8,128)S(1)}, u32[]{:S(2)}, u32[]{:S(2)}) %collective-permute-start) | collective-permute-done | bytes 262176 | tf_op jit(solution)/shard_map/while/body/eval_jaxpr/ppermute | solution.py:14
  378.7 12.2 %collective-permute-done = f32[4,128,128]{2,1,0:T(8,128)S(1)} collective-permute-done((f32[4,128,128]{2,1,0:T(8,128)}, f32[4,128,128]{2,1,0:T(8,128)S(1)}, u32[]{:S(2)}, u32[]{:S(2)}) %collective-permute-start) | collective-permute-done | bytes 262176 | tf_op jit(solution)/shard_map/while/body/eval_jaxpr/ppermute | solution.py:14
  392.5 1.9 collective-permute-start
  394.5 11.3 %collective-permute-done = f32[4,128,128]{2,1,0:T(8,128)S(1)} collective-permute-done((f32[4,128,128]{2,1,0:T(8,128)}, f32[4,128,128]{2,1,0:T(8,128)S(1)}, u32[]{:S(2)}, u32[]{:S(2)}) %collective-permute-start) | collective-permute-done | bytes 262176 | tf_op jit(solution)/shard_map/while/body/eval_jaxpr/ppermute | solution.py:14
  407.5 1.9 collective-permute-start
  409.4 10.5 %collective-permute-done = f32[4,128,128]{2,1,0:T(8,128)S(1)} collective-permute-done((f32[4,128,128]{2,1,0:T(8,128)}, f32[4,128,128]{2,1,0:T(8,128)S(1)}, u32[]{:S(2)}, u32[]{:S(2)}) %collective-permute-start) | collective-permute-done | bytes 262176 | tf_op jit(solution)/shard_map/while/body/eval_jaxpr/ppermute | solution.py:14
  421.5 1.9 collective-permute-start
  423.4 9.9 %collective-permute-done = f32[4,128,128]{2,1,0:T(8,128)S(1)} collective-permute-done((f32[4,128,128]{2,1,0:T(8,128)}, f32[4,128,128]{2,1,0:T(8,128)S(1)}, u32[]{:S(2)}, u32[]{:S(2)}) %collective-permute-start) | collective-permute-done | bytes 262176 | tf_op jit(solution)/shard_map/while/body/eval_jaxpr/ppermute | solution.py:14
  435.0 1.9 collective-permute-start
  436.9 9.9 %collective-permute-done = f32[4,128,128]{2,1,0:T(8,128)S(1)} collective-permute-done((f32[4,128,128]{2,1,0:T(8,128)}, f32[4,128,128]{2,1,0:T(8,128)S(1)}, u32[]{:S(2)}, u32[]{:S(2)}) %collective-permute-start) | collective-permute-done | bytes 262176 | tf_op jit(solution)/shard_map/while/body/eval_jaxpr/ppermute | solution.py:14
  448.4 1.9 collective-permute-start
  450.3 9.9 %collective-permute-done = f32[4,128,128]{2,1,0:T(8,128)S(1)} collective-permute-done((f32[4,128,128]{2,1,0:T(8,128)}, f32[4,128,128]{2,1,0:T(8,128)S(1)}, u32[]{:S(2)}, u32[]{:S(2)}) %collective-permute-start) | collective-permute-done | bytes 262176 | tf_op jit(solution)/shard_map/while/body/eval_jaxpr/ppermute | solution.py:14
  461.9 1.9 collective-permute-start
  463.8 9.9 %collective-permute-done = f32[4,128,128]{2,1,0:T(8,128)S(1)} collective-permute-done((f32[4,128,128]{2,1,0:T(8,128)}, f32[4,128,128]{2,1,0:T(8,128)S(1)}, u32[]{:S(2)}, u32[]{:S(2)}) %collective-permute-start) | collective-permute-done | bytes 262176 | tf_op jit(solution)/shard_map/while/body/eval_jaxpr/ppermute | solution.py:14
  477.3 9.9 %collective-permute-done = f32[4,128,128]{2,1,0:T(8,128)S(1)} collective-permute-done((f32[4,128,128]{2,1,0:T(8,128)}, f32[4,128,128]{2,1,0:T(8,128)S(1)}, u32[]{:S(2)}, u32[]{:S(2)}) %collective-permute-start) | collective-permute-done | bytes 262176 | tf_op jit(solution)/shard_map/while/body/eval_jaxpr/ppermute | solution.py:14
  487.1 2.6 fusion.4
  489.8 4.1 multiply_reduce_fusion
  493.9 2.2 multiply_convert_fusion
  496.1 2.0 copy.8
  (57 shorter events, 68.8 us)
Async XLA Ops:
  6.5 34.4 %copy-start = (bf16[3072,512]{1,0:T(8,128)(2,1)S(1)}, bf16[3072,512]{1,0:T(8,128)(2,1)}, u32[]{:S(2)}) copy-start(bf16[3072,512]{1,0:T(8,128)(2,1)} %param.10) | copy-start | bytes 9437188
  6.5 34.4 %all-gather.2.cloned.1.call-start = ((), (), s32[]{:S(2)}) async-start(), calls=%async_computation | async-start | bytes 3538944 | tf_op jit(solution)/shard_map/all_gather | solution.py:20
  41.0 3.9 copy-start.3
  41.0 3.9 copy-start.5
  44.9 1.9 copy-start.4
  48.7 1.1 copy-start.1
  52.6 13.9 %collective-permute-start = (f32[4,128,128]{2,1,0:T(8,128)}, f32[4,128,128]{2,1,0:T(8,128)S(1)}, u32[]{:S(2)}, u32[]{:S(2)}) collective-permute-start(f32[4,128,128]{2,1,0:T(8,128)} %add.39), channel_id=1, source_target_pairs={{0,8},{8,16},{16,24},{24,32},{32,40},{40,48},{48,56},{56,64},{64,7... | collective-permute-start | bytes 786440 | tf_op jit(solution)/shard_map/while/body/eval_jaxpr/ppermute | solution.py:14
  68.1 13.0 %collective-permute-start = (f32[4,128,128]{2,1,0:T(8,128)}, f32[4,128,128]{2,1,0:T(8,128)S(1)}, u32[]{:S(2)}, u32[]{:S(2)}) collective-permute-start(f32[4,128,128]{2,1,0:T(8,128)} %add.39), channel_id=1, source_target_pairs={{0,8},{8,16},{16,24},{24,32},{32,40},{40,48},{48,56},{56,64},{64,7... | collective-permute-start | bytes 786440 | tf_op jit(solution)/shard_map/while/body/eval_jaxpr/ppermute | solution.py:14
  82.8 12.1 %collective-permute-start = (f32[4,128,128]{2,1,0:T(8,128)}, f32[4,128,128]{2,1,0:T(8,128)S(1)}, u32[]{:S(2)}, u32[]{:S(2)}) collective-permute-start(f32[4,128,128]{2,1,0:T(8,128)} %add.39), channel_id=1, source_target_pairs={{0,8},{8,16},{16,24},{24,32},{32,40},{40,48},{48,56},{56,64},{64,7... | collective-permute-start | bytes 786440 | tf_op jit(solution)/shard_map/while/body/eval_jaxpr/ppermute | solution.py:14
  96.6 11.8 %collective-permute-start = (f32[4,128,128]{2,1,0:T(8,128)}, f32[4,128,128]{2,1,0:T(8,128)S(1)}, u32[]{:S(2)}, u32[]{:S(2)}) collective-permute-start(f32[4,128,128]{2,1,0:T(8,128)} %add.39), channel_id=1, source_target_pairs={{0,8},{8,16},{16,24},{24,32},{32,40},{40,48},{48,56},{56,64},{64,7... | collective-permute-start | bytes 786440 | tf_op jit(solution)/shard_map/while/body/eval_jaxpr/ppermute | solution.py:14
  110.1 11.8 %collective-permute-start = (f32[4,128,128]{2,1,0:T(8,128)}, f32[4,128,128]{2,1,0:T(8,128)S(1)}, u32[]{:S(2)}, u32[]{:S(2)}) collective-permute-start(f32[4,128,128]{2,1,0:T(8,128)} %add.39), channel_id=1, source_target_pairs={{0,8},{8,16},{16,24},{24,32},{32,40},{40,48},{48,56},{56,64},{64,7... | collective-permute-start | bytes 786440 | tf_op jit(solution)/shard_map/while/body/eval_jaxpr/ppermute | solution.py:14
  123.5 11.8 %collective-permute-start = (f32[4,128,128]{2,1,0:T(8,128)}, f32[4,128,128]{2,1,0:T(8,128)S(1)}, u32[]{:S(2)}, u32[]{:S(2)}) collective-permute-start(f32[4,128,128]{2,1,0:T(8,128)} %add.39), channel_id=1, source_target_pairs={{0,8},{8,16},{16,24},{24,32},{32,40},{40,48},{48,56},{56,64},{64,7... | collective-permute-start | bytes 786440 | tf_op jit(solution)/shard_map/while/body/eval_jaxpr/ppermute | solution.py:14
  137.0 11.8 %collective-permute-start = (f32[4,128,128]{2,1,0:T(8,128)}, f32[4,128,128]{2,1,0:T(8,128)S(1)}, u32[]{:S(2)}, u32[]{:S(2)}) collective-permute-start(f32[4,128,128]{2,1,0:T(8,128)} %add.39), channel_id=1, source_target_pairs={{0,8},{8,16},{16,24},{24,32},{32,40},{40,48},{48,56},{56,64},{64,7... | collective-permute-start | bytes 786440 | tf_op jit(solution)/shard_map/while/body/eval_jaxpr/ppermute | solution.py:14
  150.4 11.8 %collective-permute-start = (f32[4,128,128]{2,1,0:T(8,128)}, f32[4,128,128]{2,1,0:T(8,128)S(1)}, u32[]{:S(2)}, u32[]{:S(2)}) collective-permute-start(f32[4,128,128]{2,1,0:T(8,128)} %add.39), channel_id=1, source_target_pairs={{0,8},{8,16},{16,24},{24,32},{32,40},{40,48},{48,56},{56,64},{64,7... | collective-permute-start | bytes 786440 | tf_op jit(solution)/shard_map/while/body/eval_jaxpr/ppermute | solution.py:14
  163.9 11.8 %collective-permute-start = (f32[4,128,128]{2,1,0:T(8,128)}, f32[4,128,128]{2,1,0:T(8,128)S(1)}, u32[]{:S(2)}, u32[]{:S(2)}) collective-permute-start(f32[4,128,128]{2,1,0:T(8,128)} %add.39), channel_id=1, source_target_pairs={{0,8},{8,16},{16,24},{24,32},{32,40},{40,48},{48,56},{56,64},{64,7... | collective-permute-start | bytes 786440 | tf_op jit(solution)/shard_map/while/body/eval_jaxpr/ppermute | solution.py:14
  177.3 12.5 %collective-permute-start = (f32[4,128,128]{2,1,0:T(8,128)}, f32[4,128,128]{2,1,0:T(8,128)S(1)}, u32[]{:S(2)}, u32[]{:S(2)}) collective-permute-start(f32[4,128,128]{2,1,0:T(8,128)} %add.39), channel_id=1, source_target_pairs={{0,8},{8,16},{16,24},{24,32},{32,40},{40,48},{48,56},{56,64},{64,7... | collective-permute-start | bytes 786440 | tf_op jit(solution)/shard_map/while/body/eval_jaxpr/ppermute | solution.py:14
  191.5 13.6 %collective-permute-start = (f32[4,128,128]{2,1,0:T(8,128)}, f32[4,128,128]{2,1,0:T(8,128)S(1)}, u32[]{:S(2)}, u32[]{:S(2)}) collective-permute-start(f32[4,128,128]{2,1,0:T(8,128)} %add.39), channel_id=1, source_target_pairs={{0,8},{8,16},{16,24},{24,32},{32,40},{40,48},{48,56},{56,64},{64,7... | collective-permute-start | bytes 786440 | tf_op jit(solution)/shard_map/while/body/eval_jaxpr/ppermute | solution.py:14
  206.8 14.4 %collective-permute-start = (f32[4,128,128]{2,1,0:T(8,128)}, f32[4,128,128]{2,1,0:T(8,128)S(1)}, u32[]{:S(2)}, u32[]{:S(2)}) collective-permute-start(f32[4,128,128]{2,1,0:T(8,128)} %add.39), channel_id=1, source_target_pairs={{0,8},{8,16},{16,24},{24,32},{32,40},{40,48},{48,56},{56,64},{64,7... | collective-permute-start | bytes 786440 | tf_op jit(solution)/shard_map/while/body/eval_jaxpr/ppermute | solution.py:14
  222.9 13.6 %collective-permute-start = (f32[4,128,128]{2,1,0:T(8,128)}, f32[4,128,128]{2,1,0:T(8,128)S(1)}, u32[]{:S(2)}, u32[]{:S(2)}) collective-permute-start(f32[4,128,128]{2,1,0:T(8,128)} %add.39), channel_id=1, source_target_pairs={{0,8},{8,16},{16,24},{24,32},{32,40},{40,48},{48,56},{56,64},{64,7... | collective-permute-start | bytes 786440 | tf_op jit(solution)/shard_map/while/body/eval_jaxpr/ppermute | solution.py:14
  238.1 12.7 %collective-permute-start = (f32[4,128,128]{2,1,0:T(8,128)}, f32[4,128,128]{2,1,0:T(8,128)S(1)}, u32[]{:S(2)}, u32[]{:S(2)}) collective-permute-start(f32[4,128,128]{2,1,0:T(8,128)} %add.39), channel_id=1, source_target_pairs={{0,8},{8,16},{16,24},{24,32},{32,40},{40,48},{48,56},{56,64},{64,7... | collective-permute-start | bytes 786440 | tf_op jit(solution)/shard_map/while/body/eval_jaxpr/ppermute | solution.py:14
  252.5 11.8 %collective-permute-start = (f32[4,128,128]{2,1,0:T(8,128)}, f32[4,128,128]{2,1,0:T(8,128)S(1)}, u32[]{:S(2)}, u32[]{:S(2)}) collective-permute-start(f32[4,128,128]{2,1,0:T(8,128)} %add.39), channel_id=1, source_target_pairs={{0,8},{8,16},{16,24},{24,32},{32,40},{40,48},{48,56},{56,64},{64,7... | collective-permute-start | bytes 786440 | tf_op jit(solution)/shard_map/while/body/eval_jaxpr/ppermute | solution.py:14
  266.0 11.8 %collective-permute-start = (f32[4,128,128]{2,1,0:T(8,128)}, f32[4,128,128]{2,1,0:T(8,128)S(1)}, u32[]{:S(2)}, u32[]{:S(2)}) collective-permute-start(f32[4,128,128]{2,1,0:T(8,128)} %add.39), channel_id=1, source_target_pairs={{0,8},{8,16},{16,24},{24,32},{32,40},{40,48},{48,56},{56,64},{64,7... | collective-permute-start | bytes 786440 | tf_op jit(solution)/shard_map/while/body/eval_jaxpr/ppermute | solution.py:14
  279.4 11.8 %collective-permute-start = (f32[4,128,128]{2,1,0:T(8,128)}, f32[4,128,128]{2,1,0:T(8,128)S(1)}, u32[]{:S(2)}, u32[]{:S(2)}) collective-permute-start(f32[4,128,128]{2,1,0:T(8,128)} %add.39), channel_id=1, source_target_pairs={{0,8},{8,16},{16,24},{24,32},{32,40},{40,48},{48,56},{56,64},{64,7... | collective-permute-start | bytes 786440 | tf_op jit(solution)/shard_map/while/body/eval_jaxpr/ppermute | solution.py:14
  292.9 11.8 %collective-permute-start = (f32[4,128,128]{2,1,0:T(8,128)}, f32[4,128,128]{2,1,0:T(8,128)S(1)}, u32[]{:S(2)}, u32[]{:S(2)}) collective-permute-start(f32[4,128,128]{2,1,0:T(8,128)} %add.39), channel_id=1, source_target_pairs={{0,8},{8,16},{16,24},{24,32},{32,40},{40,48},{48,56},{56,64},{64,7... | collective-permute-start | bytes 786440 | tf_op jit(solution)/shard_map/while/body/eval_jaxpr/ppermute | solution.py:14
  306.3 11.8 %collective-permute-start = (f32[4,128,128]{2,1,0:T(8,128)}, f32[4,128,128]{2,1,0:T(8,128)S(1)}, u32[]{:S(2)}, u32[]{:S(2)}) collective-permute-start(f32[4,128,128]{2,1,0:T(8,128)} %add.39), channel_id=1, source_target_pairs={{0,8},{8,16},{16,24},{24,32},{32,40},{40,48},{48,56},{56,64},{64,7... | collective-permute-start | bytes 786440 | tf_op jit(solution)/shard_map/while/body/eval_jaxpr/ppermute | solution.py:14
  319.8 11.8 %collective-permute-start = (f32[4,128,128]{2,1,0:T(8,128)}, f32[4,128,128]{2,1,0:T(8,128)S(1)}, u32[]{:S(2)}, u32[]{:S(2)}) collective-permute-start(f32[4,128,128]{2,1,0:T(8,128)} %add.39), channel_id=1, source_target_pairs={{0,8},{8,16},{16,24},{24,32},{32,40},{40,48},{48,56},{56,64},{64,7... | collective-permute-start | bytes 786440 | tf_op jit(solution)/shard_map/while/body/eval_jaxpr/ppermute | solution.py:14
  333.2 11.8 %collective-permute-start = (f32[4,128,128]{2,1,0:T(8,128)}, f32[4,128,128]{2,1,0:T(8,128)S(1)}, u32[]{:S(2)}, u32[]{:S(2)}) collective-permute-start(f32[4,128,128]{2,1,0:T(8,128)} %add.39), channel_id=1, source_target_pairs={{0,8},{8,16},{16,24},{24,32},{32,40},{40,48},{48,56},{56,64},{64,7... | collective-permute-start | bytes 786440 | tf_op jit(solution)/shard_map/while/body/eval_jaxpr/ppermute | solution.py:14
  346.7 12.8 %collective-permute-start = (f32[4,128,128]{2,1,0:T(8,128)}, f32[4,128,128]{2,1,0:T(8,128)S(1)}, u32[]{:S(2)}, u32[]{:S(2)}) collective-permute-start(f32[4,128,128]{2,1,0:T(8,128)} %add.39), channel_id=1, source_target_pairs={{0,8},{8,16},{16,24},{24,32},{32,40},{40,48},{48,56},{56,64},{64,7... | collective-permute-start | bytes 786440 | tf_op jit(solution)/shard_map/while/body/eval_jaxpr/ppermute | solution.py:14
  361.2 13.9 %collective-permute-start = (f32[4,128,128]{2,1,0:T(8,128)}, f32[4,128,128]{2,1,0:T(8,128)S(1)}, u32[]{:S(2)}, u32[]{:S(2)}) collective-permute-start(f32[4,128,128]{2,1,0:T(8,128)} %add.39), channel_id=1, source_target_pairs={{0,8},{8,16},{16,24},{24,32},{32,40},{40,48},{48,56},{56,64},{64,7... | collective-permute-start | bytes 786440 | tf_op jit(solution)/shard_map/while/body/eval_jaxpr/ppermute | solution.py:14
  376.8 14.1 %collective-permute-start = (f32[4,128,128]{2,1,0:T(8,128)}, f32[4,128,128]{2,1,0:T(8,128)S(1)}, u32[]{:S(2)}, u32[]{:S(2)}) collective-permute-start(f32[4,128,128]{2,1,0:T(8,128)} %add.39), channel_id=1, source_target_pairs={{0,8},{8,16},{16,24},{24,32},{32,40},{40,48},{48,56},{56,64},{64,7... | collective-permute-start | bytes 786440 | tf_op jit(solution)/shard_map/while/body/eval_jaxpr/ppermute | solution.py:14
  392.5 13.2 %collective-permute-start = (f32[4,128,128]{2,1,0:T(8,128)}, f32[4,128,128]{2,1,0:T(8,128)S(1)}, u32[]{:S(2)}, u32[]{:S(2)}) collective-permute-start(f32[4,128,128]{2,1,0:T(8,128)} %add.39), channel_id=1, source_target_pairs={{0,8},{8,16},{16,24},{24,32},{32,40},{40,48},{48,56},{56,64},{64,7... | collective-permute-start | bytes 786440 | tf_op jit(solution)/shard_map/while/body/eval_jaxpr/ppermute | solution.py:14
  407.5 12.4 %collective-permute-start = (f32[4,128,128]{2,1,0:T(8,128)}, f32[4,128,128]{2,1,0:T(8,128)S(1)}, u32[]{:S(2)}, u32[]{:S(2)}) collective-permute-start(f32[4,128,128]{2,1,0:T(8,128)} %add.39), channel_id=1, source_target_pairs={{0,8},{8,16},{16,24},{24,32},{32,40},{40,48},{48,56},{56,64},{64,7... | collective-permute-start | bytes 786440 | tf_op jit(solution)/shard_map/while/body/eval_jaxpr/ppermute | solution.py:14
  421.5 11.8 %collective-permute-start = (f32[4,128,128]{2,1,0:T(8,128)}, f32[4,128,128]{2,1,0:T(8,128)S(1)}, u32[]{:S(2)}, u32[]{:S(2)}) collective-permute-start(f32[4,128,128]{2,1,0:T(8,128)} %add.39), channel_id=1, source_target_pairs={{0,8},{8,16},{16,24},{24,32},{32,40},{40,48},{48,56},{56,64},{64,7... | collective-permute-start | bytes 786440 | tf_op jit(solution)/shard_map/while/body/eval_jaxpr/ppermute | solution.py:14
  435.0 11.8 %collective-permute-start = (f32[4,128,128]{2,1,0:T(8,128)}, f32[4,128,128]{2,1,0:T(8,128)S(1)}, u32[]{:S(2)}, u32[]{:S(2)}) collective-permute-start(f32[4,128,128]{2,1,0:T(8,128)} %add.39), channel_id=1, source_target_pairs={{0,8},{8,16},{16,24},{24,32},{32,40},{40,48},{48,56},{56,64},{64,7... | collective-permute-start | bytes 786440 | tf_op jit(solution)/shard_map/while/body/eval_jaxpr/ppermute | solution.py:14
  448.4 11.8 %collective-permute-start = (f32[4,128,128]{2,1,0:T(8,128)}, f32[4,128,128]{2,1,0:T(8,128)S(1)}, u32[]{:S(2)}, u32[]{:S(2)}) collective-permute-start(f32[4,128,128]{2,1,0:T(8,128)} %add.39), channel_id=1, source_target_pairs={{0,8},{8,16},{16,24},{24,32},{32,40},{40,48},{48,56},{56,64},{64,7... | collective-permute-start | bytes 786440 | tf_op jit(solution)/shard_map/while/body/eval_jaxpr/ppermute | solution.py:14
  461.9 11.8 %collective-permute-start = (f32[4,128,128]{2,1,0:T(8,128)}, f32[4,128,128]{2,1,0:T(8,128)S(1)}, u32[]{:S(2)}, u32[]{:S(2)}) collective-permute-start(f32[4,128,128]{2,1,0:T(8,128)} %add.39), channel_id=1, source_target_pairs={{0,8},{8,16},{16,24},{24,32},{32,40},{40,48},{48,56},{56,64},{64,7... | collective-permute-start | bytes 786440 | tf_op jit(solution)/shard_map/while/body/eval_jaxpr/ppermute | solution.py:14
  475.3 11.8 %collective-permute-start = (f32[4,128,128]{2,1,0:T(8,128)}, f32[4,128,128]{2,1,0:T(8,128)S(1)}, u32[]{:S(2)}, u32[]{:S(2)}) collective-permute-start(f32[4,128,128]{2,1,0:T(8,128)} %add.39), channel_id=1, source_target_pairs={{0,8},{8,16},{16,24},{24,32},{32,40},{40,48},{48,56},{56,64},{64,7... | collective-permute-start | bytes 786440 | tf_op jit(solution)/shard_map/while/body/eval_jaxpr/ppermute | solution.py:14
  489.8 4.2 copy-start.2
Sparse Core Ops, SparseCore 0:
  9.2 31.7 all-gather.1
where the time goes:
time: 507 us; the launch traced here: 505 us
  waiting for transfers between devices  357 us (70%)
  starting transfers between devices  60.6 us (12%)
  other arithmetic  54.9 us (11%)
  matrix products  15.3 us (3%)
  between operations  13.5 us (3%)
    ppermute x31, waiting for transfers between devices, from_behind(): return lax.ppermute(value, axis, pairs)  323 us
    ppermute x31, starting transfers between devices, from_behind(): return lax.ppermute(value, axis, pairs)  60.6 us
    add x31, other arithmetic, advance(): return from_behind(carried + local_state, 'ctx', 1)  51.8 us
    all_gather x1, waiting for transfers between devices, body(): piece_rows = lax.all_gather(tokens, 'tp', axis=0, tiled=True)  32.9 us
  transfers between devices with their start and end apart: 32, of which 32 were waited for; matrix products, arithmetic and copies ran while one was open for 0% of the time, Pallas kernels for 0%

commit v1 on v0

--- a/solution.py
+++ b/solution.py
@@ -6,6 +6,13 @@
 HEAD_DIM = 128
 BLOCK = 512
 EPSILON = 1e-06
+
+
+def state_sites_in(array_dim, own_rows, chip_axis):
+    local_now = lax.axis_size(chip_axis)
+    right_arr = jnp.stack(local_now * [own_rows])
+    all_values = lax.all_to_all(right_arr, chip_axis, 0, 0)
+    return jnp.concatenate(all_values, axis=array_dim)
 
 
 def from_behind(value, axis, by):
@@ -17,7 +24,7 @@
 def body(tokens, w_query, w_key, w_value, norm_gain):
     local_width = w_query.shape[1]
     head_count = local_width // HEAD_DIM
-    piece_rows = lax.all_gather(tokens, "tp", axis=0, tiled=True)
+    piece_rows = state_sites_in(0, tokens, "tp")
     query_part = jnp.dot(piece_rows, w_query, preferred_element_type=jnp.float32).astype(
         jnp.bfloat16
     )

time: 507 us -> 508 us (level)
  between operations: 13.5 us -> 0.08 us
    all_to_all x0 -> x1, waiting for transfers between devices: none -> 37.7 us  [state_sites_in(): all_values = lax.all_to_all(right_arr, chip_axis, 0, 0)]
    all_gather x1 -> x0, waiting for transfers between devices: 32.9 us -> none  [body(): piece_rows = lax.all_gather(tokens, 'tp', axis=0, tiled=True)]
where the time goes in v1:
time: 508 us; the launch traced here: 506 us
  waiting for transfers between devices  360 us (71%)
  starting transfers between devices  65.1 us (13%)
  other arithmetic  54.7 us (11%)
  matrix products  19.3 us (4%)
  local copies, waits for them, and re-layouts  6.43 us (1%)
    ppermute x31, waiting for transfers between devices, from_behind(): return lax.ppermute(value, axis, pairs)  322 us
    ppermute x31, starting transfers between devices, from_behind(): return lax.ppermute(value, axis, pairs)  60.6 us
    add x31, other arithmetic, advance(): return from_behind(carried + local_state, 'ctx', 1)  51.6 us
    all_to_all x1, waiting for transfers between devices, state_sites_in(): all_values = lax.all_to_all(right_arr, chip_axis, 0, 0)  37.7 us
  transfers between devices with their start and end apart: 32, of which 32 were waited for; matrix products, arithmetic and copies ran while one was open for 0% of the time, Pallas kernels for 0%

profile of v1, /device:TPU:128, one launch (start us, length us, event | category | flops | bytes accessed | tf_op | source)
XLA Modules:
  0.0 505.9 jit_solution(10948354393140883473)
XLA Ops:
  0.0 3.2 stack.2
  3.2 4.5 all-to-all-start
  8.4 37.7 %all-to-all-done = bf16[8,64,3072]{2,1,0:T(8,128)(2,1)} async-done(((bf16[8,64,3072]{2,1,0:T(8,128)(2,1)}), bf16[8,64,3072]{2,1,0:T(8,128)(2,1)}, u32[]{:S(2)}, u32[]{:S(2)}) %all-to-all-start) | async-done | bytes 3145760 | tf_op jit(solution)/shard_map/all_to_all | solution.py:14
  46.2 3.9 convolution_convert_fusion
  50.1 3.9 convolution_convert_fusion.1
  54.0 3.8 convolution_convert_fusion.2
  60.1 434.8 %while.10 = (s32[]{:T(128)}, f32[4,128,128]{2,1,0:T(8,128)S(1)}, f32[4,128,128]{2,1,0:T(8,128)}, s32[]{:T(128)}) while((s32[]{:T(128)}, f32[4,128,128]{2,1,0:T(8,128)S(1)}, f32[4,128,128]{2,1,0:T(8,128)}, s32[]{:T(128)}) %tuple.19), condition=%wide.region_1.0_spmd, body=%wide.region_0.0_spmd.sunk | while | flops 65538 | bytes 1835101 | solution.py:51
  61.7 3.4 collective-permute-start
  65.1 9.8 %collective-permute-done = f32[4,128,128]{2,1,0:T(8,128)S(1)} collective-permute-done((f32[4,128,128]{2,1,0:T(8,128)}, f32[4,128,128]{2,1,0:T(8,128)S(1)}, u32[]{:S(2)}, u32[]{:S(2)}) %collective-permute-start) | collective-permute-done | bytes 262176 | tf_op jit(solution)/shard_map/while/body/eval_jaxpr/ppermute | solution.py:21
  76.6 1.9 collective-permute-start
  78.5 10.4 %collective-permute-done = f32[4,128,128]{2,1,0:T(8,128)S(1)} collective-permute-done((f32[4,128,128]{2,1,0:T(8,128)}, f32[4,128,128]{2,1,0:T(8,128)S(1)}, u32[]{:S(2)}, u32[]{:S(2)}) %collective-permute-start) | collective-permute-done | bytes 262176 | tf_op jit(solution)/shard_map/while/body/eval_jaxpr/ppermute | solution.py:21
  92.5 9.9 %collective-permute-done = f32[4,128,128]{2,1,0:T(8,128)S(1)} collective-permute-done((f32[4,128,128]{2,1,0:T(8,128)}, f32[4,128,128]{2,1,0:T(8,128)S(1)}, u32[]{:S(2)}, u32[]{:S(2)}) %collective-permute-start) | collective-permute-done | bytes 262176 | tf_op jit(solution)/shard_map/while/body/eval_jaxpr/ppermute | solution.py:21
  104.0 1.9 collective-permute-start
  105.9 9.9 %collective-permute-done = f32[4,128,128]{2,1,0:T(8,128)S(1)} collective-permute-done((f32[4,128,128]{2,1,0:T(8,128)}, f32[4,128,128]{2,1,0:T(8,128)S(1)}, u32[]{:S(2)}, u32[]{:S(2)}) %collective-permute-start) | collective-permute-done | bytes 262176 | tf_op jit(solution)/shard_map/while/body/eval_jaxpr/ppermute | solution.py:21
  117.5 1.9 collective-permute-start
  119.4 9.9 %collective-permute-done = f32[4,128,128]{2,1,0:T(8,128)S(1)} collective-permute-done((f32[4,128,128]{2,1,0:T(8,128)}, f32[4,128,128]{2,1,0:T(8,128)S(1)}, u32[]{:S(2)}, u32[]{:S(2)}) %collective-permute-start) | collective-permute-done | bytes 262176 | tf_op jit(solution)/shard_map/while/body/eval_jaxpr/ppermute | solution.py:21
  132.8 9.9 %collective-permute-done = f32[4,128,128]{2,1,0:T(8,128)S(1)} collective-permute-done((f32[4,128,128]{2,1,0:T(8,128)}, f32[4,128,128]{2,1,0:T(8,128)S(1)}, u32[]{:S(2)}, u32[]{:S(2)}) %collective-permute-start) | collective-permute-done | bytes 262176 | tf_op jit(solution)/shard_map/while/body/eval_jaxpr/ppermute | solution.py:21
  144.3 1.9 collective-permute-start
  146.3 9.9 %collective-permute-done = f32[4,128,128]{2,1,0:T(8,128)S(1)} collective-permute-done((f32[4,128,128]{2,1,0:T(8,128)}, f32[4,128,128]{2,1,0:T(8,128)S(1)}, u32[]{:S(2)}, u32[]{:S(2)}) %collective-permute-start) | collective-permute-done | bytes 262176 | tf_op jit(solution)/shard_map/while/body/eval_jaxpr/ppermute | solution.py:21
  157.8 1.9 collective-permute-start
  159.7 9.9 %collective-permute-done = f32[4,128,128]{2,1,0:T(8,128)S(1)} collective-permute-done((f32[4,128,128]{2,1,0:T(8,128)}, f32[4,128,128]{2,1,0:T(8,128)S(1)}, u32[]{:S(2)}, u32[]{:S(2)}) %collective-permute-start) | collective-permute-done | bytes 262176 | tf_op jit(solution)/shard_map/while/body/eval_jaxpr/ppermute | solution.py:21
  171.2 1.9 collective-permute-start
  173.2 10.4 %collective-permute-done = f32[4,128,128]{2,1,0:T(8,128)S(1)} collective-permute-done((f32[4,128,128]{2,1,0:T(8,128)}, f32[4,128,128]{2,1,0:T(8,128)S(1)}, u32[]{:S(2)}, u32[]{:S(2)}) %collective-permute-start) | collective-permute-done | bytes 262176 | tf_op jit(solution)/shard_map/while/body/eval_jaxpr/ppermute | solution.py:21
  185.2 1.9 collective-permute-start
  187.2 11.5 %collective-permute-done = f32[4,128,128]{2,1,0:T(8,128)S(1)} collective-permute-done((f32[4,128,128]{2,1,0:T(8,128)}, f32[4,128,128]{2,1,0:T(8,128)S(1)}, u32[]{:S(2)}, u32[]{:S(2)}) %collective-permute-start) | collective-permute-done | bytes 262176 | tf_op jit(solution)/shard_map/while/body/eval_jaxpr/ppermute | solution.py:21
  200.4 1.9 collective-permute-start
  202.3 12.6 %collective-permute-done = f32[4,128,128]{2,1,0:T(8,128)S(1)} collective-permute-done((f32[4,128,128]{2,1,0:T(8,128)}, f32[4,128,128]{2,1,0:T(8,128)S(1)}, u32[]{:S(2)}, u32[]{:S(2)}) %collective-permute-start) | collective-permute-done | bytes 262176 | tf_op jit(solution)/shard_map/while/body/eval_jaxpr/ppermute | solution.py:21
  218.5 11.8 %collective-permute-done = f32[4,128,128]{2,1,0:T(8,128)S(1)} collective-permute-done((f32[4,128,128]{2,1,0:T(8,128)}, f32[4,128,128]{2,1,0:T(8,128)S(1)}, u32[]{:S(2)}, u32[]{:S(2)}) %collective-permute-start) | collective-permute-done | bytes 262176 | tf_op jit(solution)/shard_map/while/body/eval_jaxpr/ppermute | solution.py:21
  232.0 1.9 collective-permute-start
  233.9 10.9 %collective-permute-done = f32[4,128,128]{2,1,0:T(8,128)S(1)} collective-permute-done((f32[4,128,128]{2,1,0:T(8,128)}, f32[4,128,128]{2,1,0:T(8,128)S(1)}, u32[]{:S(2)}, u32[]{:S(2)}) %collective-permute-start) | collective-permute-done | bytes 262176 | tf_op jit(solution)/shard_map/while/body/eval_jaxpr/ppermute | solution.py:21
  248.4 10.1 %collective-permute-done = f32[4,128,128]{2,1,0:T(8,128)S(1)} collective-permute-done((f32[4,128,128]{2,1,0:T(8,128)}, f32[4,128,128]{2,1,0:T(8,128)S(1)}, u32[]{:S(2)}, u32[]{:S(2)}) %collective-permute-start) | collective-permute-done | bytes 262176 | tf_op jit(solution)/shard_map/while/body/eval_jaxpr/ppermute | solution.py:21
  262.1 9.9 %collective-permute-done = f32[4,128,128]{2,1,0:T(8,128)S(1)} collective-permute-done((f32[4,128,128]{2,1,0:T(8,128)}, f32[4,128,128]{2,1,0:T(8,128)S(1)}, u32[]{:S(2)}, u32[]{:S(2)}) %collective-permute-start) | collective-permute-done | bytes 262176 | tf_op jit(solution)/shard_map/while/body/eval_jaxpr/ppermute | solution.py:21
  273.6 1.9 collective-permute-start
  275.5 9.9 %collective-permute-done = f32[4,128,128]{2,1,0:T(8,128)S(1)} collective-permute-done((f32[4,128,128]{2,1,0:T(8,128)}, f32[4,128,128]{2,1,0:T(8,128)S(1)}, u32[]{:S(2)}, u32[]{:S(2)}) %collective-permute-start) | collective-permute-done | bytes 262176 | tf_op jit(solution)/shard_map/while/body/eval_jaxpr/ppermute | solution.py:21
  287.1 1.9 collective-permute-start
  289.0 9.9 %collective-permute-done = f32[4,128,128]{2,1,0:T(8,128)S(1)} collective-permute-done((f32[4,128,128]{2,1,0:T(8,128)}, f32[4,128,128]{2,1,0:T(8,128)S(1)}, u32[]{:S(2)}, u32[]{:S(2)}) %collective-permute-start) | collective-permute-done | bytes 262176 | tf_op jit(solution)/shard_map/while/body/eval_jaxpr/ppermute | solution.py:21
  302.4 9.9 %collective-permute-done = f32[4,128,128]{2,1,0:T(8,128)S(1)} collective-permute-done((f32[4,128,128]{2,1,0:T(8,128)}, f32[4,128,128]{2,1,0:T(8,128)S(1)}, u32[]{:S(2)}, u32[]{:S(2)}) %collective-permute-start) | collective-permute-done | bytes 262176 | tf_op jit(solution)/shard_map/while/body/eval_jaxpr/ppermute | solution.py:21
  314.0 1.9 collective-permute-start
  315.9 9.9 %collective-permute-done = f32[4,128,128]{2,1,0:T(8,128)S(1)} collective-permute-done((f32[4,128,128]{2,1,0:T(8,128)}, f32[4,128,128]{2,1,0:T(8,128)S(1)}, u32[]{:S(2)}, u32[]{:S(2)}) %collective-permute-start) | collective-permute-done | bytes 262176 | tf_op jit(solution)/shard_map/while/body/eval_jaxpr/ppermute | solution.py:21
  327.4 1.9 collective-permute-start
  329.3 9.9 %collective-permute-done = f32[4,128,128]{2,1,0:T(8,128)S(1)} collective-permute-done((f32[4,128,128]{2,1,0:T(8,128)}, f32[4,128,128]{2,1,0:T(8,128)S(1)}, u32[]{:S(2)}, u32[]{:S(2)}) %collective-permute-start) | collective-permute-done | bytes 262176 | tf_op jit(solution)/shard_map/while/body/eval_jaxpr/ppermute | solution.py:21
  342.8 10.7 %collective-permute-done = f32[4,128,128]{2,1,0:T(8,128)S(1)} collective-permute-done((f32[4,128,128]{2,1,0:T(8,128)}, f32[4,128,128]{2,1,0:T(8,128)S(1)}, u32[]{:S(2)}, u32[]{:S(2)}) %collective-permute-start) | collective-permute-done | bytes 262176 | tf_op jit(solution)/shard_map/while/body/eval_jaxpr/ppermute | solution.py:21
  357.1 11.9 %collective-permute-done = f32[4,128,128]{2,1,0:T(8,128)S(1)} collective-permute-done((f32[4,128,128]{2,1,0:T(8,128)}, f32[4,128,128]{2,1,0:T(8,128)S(1)}, u32[]{:S(2)}, u32[]{:S(2)}) %collective-permute-start) | collective-permute-done | bytes 262176 | tf_op jit(solution)/shard_map/while/body/eval_jaxpr/ppermute | solution.py:21
  370.6 1.9 collective-permute-start
  372.5 12.3 %collective-permute-done = f32[4,128,128]{2,1,0:T(8,128)S(1)} collective-permute-done((f32[4,128,128]{2,1,0:T(8,128)}, f32[4,128,128]{2,1,0:T(8,128)S(1)}, u32[]{:S(2)}, u32[]{:S(2)}) %collective-permute-start) | collective-permute-done | bytes 262176 | tf_op jit(solution)/shard_map/while/body/eval_jaxpr/ppermute | solution.py:21
  386.5 1.9 collective-permute-start
  388.4 11.5 %collective-permute-done = f32[4,128,128]{2,1,0:T(8,128)S(1)} collective-permute-done((f32[4,128,128]{2,1,0:T(8,128)}, f32[4,128,128]{2,1,0:T(8,128)S(1)}, u32[]{:S(2)}, u32[]{:S(2)}) %collective-permute-start) | collective-permute-done | bytes 262176 | tf_op jit(solution)/shard_map/while/body/eval_jaxpr/ppermute | solution.py:21
  401.6 1.9 collective-permute-start
  403.5 10.6 %collective-permute-done = f32[4,128,128]{2,1,0:T(8,128)S(1)} collective-permute-done((f32[4,128,128]{2,1,0:T(8,128)}, f32[4,128,128]{2,1,0:T(8,128)S(1)}, u32[]{:S(2)}, u32[]{:S(2)}) %collective-permute-start) | collective-permute-done | bytes 262176 | tf_op jit(solution)/shard_map/while/body/eval_jaxpr/ppermute | solution.py:21
  415.8 1.9 collective-permute-start
  417.7 9.9 %collective-permute-done = f32[4,128,128]{2,1,0:T(8,128)S(1)} collective-permute-done((f32[4,128,128]{2,1,0:T(8,128)}, f32[4,128,128]{2,1,0:T(8,128)S(1)}, u32[]{:S(2)}, u32[]{:S(2)}) %collective-permute-start) | collective-permute-done | bytes 262176 | tf_op jit(solution)/shard_map/while/body/eval_jaxpr/ppermute | solution.py:21
  431.2 9.9 %collective-permute-done = f32[4,128,128]{2,1,0:T(8,128)S(1)} collective-permute-done((f32[4,128,128]{2,1,0:T(8,128)}, f32[4,128,128]{2,1,0:T(8,128)S(1)}, u32[]{:S(2)}, u32[]{:S(2)}) %collective-permute-start) | collective-permute-done | bytes 262176 | tf_op jit(solution)/shard_map/while/body/eval_jaxpr/ppermute | solution.py:21
  442.7 1.9 collective-permute-start
  444.6 9.9 %collective-permute-done = f32[4,128,128]{2,1,0:T(8,128)S(1)} collective-permute-done((f32[4,128,128]{2,1,0:T(8,128)}, f32[4,128,128]{2,1,0:T(8,128)S(1)}, u32[]{:S(2)}, u32[]{:S(2)}) %collective-permute-start) | collective-permute-done | bytes 262176 | tf_op jit(solution)/shard_map/while/body/eval_jaxpr/ppermute | solution.py:21
  456.1 1.9 collective-permute-start
  458.1 9.9 %collective-permute-done = f32[4,128,128]{2,1,0:T(8,128)S(1)} collective-permute-done((f32[4,128,128]{2,1,0:T(8,128)}, f32[4,128,128]{2,1,0:T(8,128)S(1)}, u32[]{:S(2)}, u32[]{:S(2)}) %collective-permute-start) | collective-permute-done | bytes 262176 | tf_op jit(solution)/shard_map/while/body/eval_jaxpr/ppermute | solution.py:21
  469.6 1.9 collective-permute-start
  471.5 9.9 %collective-permute-done = f32[4,128,128]{2,1,0:T(8,128)S(1)} collective-permute-done((f32[4,128,128]{2,1,0:T(8,128)}, f32[4,128,128]{2,1,0:T(8,128)S(1)}, u32[]{:S(2)}, u32[]{:S(2)}) %collective-permute-start) | collective-permute-done | bytes 262176 | tf_op jit(solution)/shard_map/while/body/eval_jaxpr/ppermute | solution.py:21
  483.0 1.9 collective-permute-start
  485.0 9.9 %collective-permute-done = f32[4,128,128]{2,1,0:T(8,128)S(1)} collective-permute-done((f32[4,128,128]{2,1,0:T(8,128)}, f32[4,128,128]{2,1,0:T(8,128)S(1)}, u32[]{:S(2)}, u32[]{:S(2)}) %collective-permute-start) | collective-permute-done | bytes 262176 | tf_op jit(solution)/shard_map/while/body/eval_jaxpr/ppermute | solution.py:21
  494.8 2.6 fusion.4
  497.5 4.2 multiply_reduce_fusion
  501.7 2.2 multiply_convert_fusion
  503.8 2.0 copy.8
  (55 shorter events, 71.8 us)
Async XLA Ops:
  0.0 46.2 %copy-start = (bf16[3072,512]{1,0:T(8,128)(2,1)S(1)}, bf16[3072,512]{1,0:T(8,128)(2,1)}, u32[]{:S(2)}) copy-start(bf16[3072,512]{1,0:T(8,128)(2,1)} %param.10) | copy-start | bytes 9437188
  3.2 43.0 %all-to-all-start = ((bf16[8,64,3072]{2,1,0:T(8,128)(2,1)}), bf16[8,64,3072]{2,1,0:T(8,128)(2,1)}, u32[]{:S(2)}, u32[]{:S(2)}) async-start(bf16[8,64,3072]{2,1,0:T(8,128)(2,1)} %stack.2), calls=%async_computation | async-start | bytes 6291456 | tf_op jit(solution)/shard_map/all_to_all | solution.py:14
  46.2 3.9 copy-start.3
  50.1 3.9 copy-start.4
  57.9 1.1 copy-start.1
  61.7 13.2 %collective-permute-start = (f32[4,128,128]{2,1,0:T(8,128)}, f32[4,128,128]{2,1,0:T(8,128)S(1)}, u32[]{:S(2)}, u32[]{:S(2)}) collective-permute-start(f32[4,128,128]{2,1,0:T(8,128)} %add.39), channel_id=1, source_target_pairs={{0,8},{8,16},{16,24},{24,32},{32,40},{40,48},{48,56},{56,64},{64,7... | collective-permute-start | bytes 786440 | tf_op jit(solution)/shard_map/while/body/eval_jaxpr/ppermute | solution.py:21
  76.6 12.3 %collective-permute-start = (f32[4,128,128]{2,1,0:T(8,128)}, f32[4,128,128]{2,1,0:T(8,128)S(1)}, u32[]{:S(2)}, u32[]{:S(2)}) collective-permute-start(f32[4,128,128]{2,1,0:T(8,128)} %add.39), channel_id=1, source_target_pairs={{0,8},{8,16},{16,24},{24,32},{32,40},{40,48},{48,56},{56,64},{64,7... | collective-permute-start | bytes 786440 | tf_op jit(solution)/shard_map/while/body/eval_jaxpr/ppermute | solution.py:21
  90.6 11.8 %collective-permute-start = (f32[4,128,128]{2,1,0:T(8,128)}, f32[4,128,128]{2,1,0:T(8,128)S(1)}, u32[]{:S(2)}, u32[]{:S(2)}) collective-permute-start(f32[4,128,128]{2,1,0:T(8,128)} %add.39), channel_id=1, source_target_pairs={{0,8},{8,16},{16,24},{24,32},{32,40},{40,48},{48,56},{56,64},{64,7... | collective-permute-start | bytes 786440 | tf_op jit(solution)/shard_map/while/body/eval_jaxpr/ppermute | solution.py:21
  104.0 11.8 %collective-permute-start = (f32[4,128,128]{2,1,0:T(8,128)}, f32[4,128,128]{2,1,0:T(8,128)S(1)}, u32[]{:S(2)}, u32[]{:S(2)}) collective-permute-start(f32[4,128,128]{2,1,0:T(8,128)} %add.39), channel_id=1, source_target_pairs={{0,8},{8,16},{16,24},{24,32},{32,40},{40,48},{48,56},{56,64},{64,7... | collective-permute-start | bytes 786440 | tf_op jit(solution)/shard_map/while/body/eval_jaxpr/ppermute | solution.py:21
  117.5 11.8 %collective-permute-start = (f32[4,128,128]{2,1,0:T(8,128)}, f32[4,128,128]{2,1,0:T(8,128)S(1)}, u32[]{:S(2)}, u32[]{:S(2)}) collective-permute-start(f32[4,128,128]{2,1,0:T(8,128)} %add.39), channel_id=1, source_target_pairs={{0,8},{8,16},{16,24},{24,32},{32,40},{40,48},{48,56},{56,64},{64,7... | collective-permute-start | bytes 786440 | tf_op jit(solution)/shard_map/while/body/eval_jaxpr/ppermute | solution.py:21
  130.9 11.8 %collective-permute-start = (f32[4,128,128]{2,1,0:T(8,128)}, f32[4,128,128]{2,1,0:T(8,128)S(1)}, u32[]{:S(2)}, u32[]{:S(2)}) collective-permute-start(f32[4,128,128]{2,1,0:T(8,128)} %add.39), channel_id=1, source_target_pairs={{0,8},{8,16},{16,24},{24,32},{32,40},{40,48},{48,56},{56,64},{64,7... | collective-permute-start | bytes 786440 | tf_op jit(solution)/shard_map/while/body/eval_jaxpr/ppermute | solution.py:21
  144.3 11.8 %collective-permute-start = (f32[4,128,128]{2,1,0:T(8,128)}, f32[4,128,128]{2,1,0:T(8,128)S(1)}, u32[]{:S(2)}, u32[]{:S(2)}) collective-permute-start(f32[4,128,128]{2,1,0:T(8,128)} %add.39), channel_id=1, source_target_pairs={{0,8},{8,16},{16,24},{24,32},{32,40},{40,48},{48,56},{56,64},{64,7... | collective-permute-start | bytes 786440 | tf_op jit(solution)/shard_map/while/body/eval_jaxpr/ppermute | solution.py:21
  157.8 11.8 %collective-permute-start = (f32[4,128,128]{2,1,0:T(8,128)}, f32[4,128,128]{2,1,0:T(8,128)S(1)}, u32[]{:S(2)}, u32[]{:S(2)}) collective-permute-start(f32[4,128,128]{2,1,0:T(8,128)} %add.39), channel_id=1, source_target_pairs={{0,8},{8,16},{16,24},{24,32},{32,40},{40,48},{48,56},{56,64},{64,7... | collective-permute-start | bytes 786440 | tf_op jit(solution)/shard_map/while/body/eval_jaxpr/ppermute | solution.py:21
  171.2 12.3 %collective-permute-start = (f32[4,128,128]{2,1,0:T(8,128)}, f32[4,128,128]{2,1,0:T(8,128)S(1)}, u32[]{:S(2)}, u32[]{:S(2)}) collective-permute-start(f32[4,128,128]{2,1,0:T(8,128)} %add.39), channel_id=1, source_target_pairs={{0,8},{8,16},{16,24},{24,32},{32,40},{40,48},{48,56},{56,64},{64,7... | collective-permute-start | bytes 786440 | tf_op jit(solution)/shard_map/while/body/eval_jaxpr/ppermute | solution.py:21
  185.2 13.5 %collective-permute-start = (f32[4,128,128]{2,1,0:T(8,128)}, f32[4,128,128]{2,1,0:T(8,128)S(1)}, u32[]{:S(2)}, u32[]{:S(2)}) collective-permute-start(f32[4,128,128]{2,1,0:T(8,128)} %add.39), channel_id=1, source_target_pairs={{0,8},{8,16},{16,24},{24,32},{32,40},{40,48},{48,56},{56,64},{64,7... | collective-permute-start | bytes 786440 | tf_op jit(solution)/shard_map/while/body/eval_jaxpr/ppermute | solution.py:21
  200.4 14.6 %collective-permute-start = (f32[4,128,128]{2,1,0:T(8,128)}, f32[4,128,128]{2,1,0:T(8,128)S(1)}, u32[]{:S(2)}, u32[]{:S(2)}) collective-permute-start(f32[4,128,128]{2,1,0:T(8,128)} %add.39), channel_id=1, source_target_pairs={{0,8},{8,16},{16,24},{24,32},{32,40},{40,48},{48,56},{56,64},{64,7... | collective-permute-start | bytes 786440 | tf_op jit(solution)/shard_map/while/body/eval_jaxpr/ppermute | solution.py:21
  216.6 13.7 %collective-permute-start = (f32[4,128,128]{2,1,0:T(8,128)}, f32[4,128,128]{2,1,0:T(8,128)S(1)}, u32[]{:S(2)}, u32[]{:S(2)}) collective-permute-start(f32[4,128,128]{2,1,0:T(8,128)} %add.39), channel_id=1, source_target_pairs={{0,8},{8,16},{16,24},{24,32},{32,40},{40,48},{48,56},{56,64},{64,7... | collective-permute-start | bytes 786440 | tf_op jit(solution)/shard_map/while/body/eval_jaxpr/ppermute | solution.py:21
  232.0 12.9 %collective-permute-start = (f32[4,128,128]{2,1,0:T(8,128)}, f32[4,128,128]{2,1,0:T(8,128)S(1)}, u32[]{:S(2)}, u32[]{:S(2)}) collective-permute-start(f32[4,128,128]{2,1,0:T(8,128)} %add.39), channel_id=1, source_target_pairs={{0,8},{8,16},{16,24},{24,32},{32,40},{40,48},{48,56},{56,64},{64,7... | collective-permute-start | bytes 786440 | tf_op jit(solution)/shard_map/while/body/eval_jaxpr/ppermute | solution.py:21
  246.5 12.0 %collective-permute-start = (f32[4,128,128]{2,1,0:T(8,128)}, f32[4,128,128]{2,1,0:T(8,128)S(1)}, u32[]{:S(2)}, u32[]{:S(2)}) collective-permute-start(f32[4,128,128]{2,1,0:T(8,128)} %add.39), channel_id=1, source_target_pairs={{0,8},{8,16},{16,24},{24,32},{32,40},{40,48},{48,56},{56,64},{64,7... | collective-permute-start | bytes 786440 | tf_op jit(solution)/shard_map/while/body/eval_jaxpr/ppermute | solution.py:21
  260.2 11.8 %collective-permute-start = (f32[4,128,128]{2,1,0:T(8,128)}, f32[4,128,128]{2,1,0:T(8,128)S(1)}, u32[]{:S(2)}, u32[]{:S(2)}) collective-permute-start(f32[4,128,128]{2,1,0:T(8,128)} %add.39), channel_id=1, source_target_pairs={{0,8},{8,16},{16,24},{24,32},{32,40},{40,48},{48,56},{56,64},{64,7... | collective-permute-start | bytes 786440 | tf_op jit(solution)/shard_map/while/body/eval_jaxpr/ppermute | solution.py:21
  273.6 11.8 %collective-permute-start = (f32[4,128,128]{2,1,0:T(8,128)}, f32[4,128,128]{2,1,0:T(8,128)S(1)}, u32[]{:S(2)}, u32[]{:S(2)}) collective-permute-start(f32[4,128,128]{2,1,0:T(8,128)} %add.39), channel_id=1, source_target_pairs={{0,8},{8,16},{16,24},{24,32},{32,40},{40,48},{48,56},{56,64},{64,7... | collective-permute-start | bytes 786440 | tf_op jit(solution)/shard_map/while/body/eval_jaxpr/ppermute | solution.py:21
  287.1 11.8 %collective-permute-start = (f32[4,128,128]{2,1,0:T(8,128)}, f32[4,128,128]{2,1,0:T(8,128)S(1)}, u32[]{:S(2)}, u32[]{:S(2)}) collective-permute-start(f32[4,128,128]{2,1,0:T(8,128)} %add.39), channel_id=1, source_target_pairs={{0,8},{8,16},{16,24},{24,32},{32,40},{40,48},{48,56},{56,64},{64,7... | collective-permute-start | bytes 786440 | tf_op jit(solution)/shard_map/while/body/eval_jaxpr/ppermute | solution.py:21
  300.5 11.8 %collective-permute-start = (f32[4,128,128]{2,1,0:T(8,128)}, f32[4,128,128]{2,1,0:T(8,128)S(1)}, u32[]{:S(2)}, u32[]{:S(2)}) collective-permute-start(f32[4,128,128]{2,1,0:T(8,128)} %add.39), channel_id=1, source_target_pairs={{0,8},{8,16},{16,24},{24,32},{32,40},{40,48},{48,56},{56,64},{64,7... | collective-permute-start | bytes 786440 | tf_op jit(solution)/shard_map/while/body/eval_jaxpr/ppermute | solution.py:21
  314.0 11.8 %collective-permute-start = (f32[4,128,128]{2,1,0:T(8,128)}, f32[4,128,128]{2,1,0:T(8,128)S(1)}, u32[]{:S(2)}, u32[]{:S(2)}) collective-permute-start(f32[4,128,128]{2,1,0:T(8,128)} %add.39), channel_id=1, source_target_pairs={{0,8},{8,16},{16,24},{24,32},{32,40},{40,48},{48,56},{56,64},{64,7... | collective-permute-start | bytes 786440 | tf_op jit(solution)/shard_map/while/body/eval_jaxpr/ppermute | solution.py:21
  327.4 11.8 %collective-permute-start = (f32[4,128,128]{2,1,0:T(8,128)}, f32[4,128,128]{2,1,0:T(8,128)S(1)}, u32[]{:S(2)}, u32[]{:S(2)}) collective-permute-start(f32[4,128,128]{2,1,0:T(8,128)} %add.39), channel_id=1, source_target_pairs={{0,8},{8,16},{16,24},{24,32},{32,40},{40,48},{48,56},{56,64},{64,7... | collective-permute-start | bytes 786440 | tf_op jit(solution)/shard_map/while/body/eval_jaxpr/ppermute | solution.py:21
  340.9 12.6 %collective-permute-start = (f32[4,128,128]{2,1,0:T(8,128)}, f32[4,128,128]{2,1,0:T(8,128)S(1)}, u32[]{:S(2)}, u32[]{:S(2)}) collective-permute-start(f32[4,128,128]{2,1,0:T(8,128)} %add.39), channel_id=1, source_target_pairs={{0,8},{8,16},{16,24},{24,32},{32,40},{40,48},{48,56},{56,64},{64,7... | collective-permute-start | bytes 786440 | tf_op jit(solution)/shard_map/while/body/eval_jaxpr/ppermute | solution.py:21
  355.2 13.8 %collective-permute-start = (f32[4,128,128]{2,1,0:T(8,128)}, f32[4,128,128]{2,1,0:T(8,128)S(1)}, u32[]{:S(2)}, u32[]{:S(2)}) collective-permute-start(f32[4,128,128]{2,1,0:T(8,128)} %add.39), channel_id=1, source_target_pairs={{0,8},{8,16},{16,24},{24,32},{32,40},{40,48},{48,56},{56,64},{64,7... | collective-permute-start | bytes 786440 | tf_op jit(solution)/shard_map/while/body/eval_jaxpr/ppermute | solution.py:21
  370.6 14.3 %collective-permute-start = (f32[4,128,128]{2,1,0:T(8,128)}, f32[4,128,128]{2,1,0:T(8,128)S(1)}, u32[]{:S(2)}, u32[]{:S(2)}) collective-permute-start(f32[4,128,128]{2,1,0:T(8,128)} %add.39), channel_id=1, source_target_pairs={{0,8},{8,16},{16,24},{24,32},{32,40},{40,48},{48,56},{56,64},{64,7... | collective-permute-start | bytes 786440 | tf_op jit(solution)/shard_map/while/body/eval_jaxpr/ppermute | solution.py:21
  386.5 13.4 %collective-permute-start = (f32[4,128,128]{2,1,0:T(8,128)}, f32[4,128,128]{2,1,0:T(8,128)S(1)}, u32[]{:S(2)}, u32[]{:S(2)}) collective-permute-start(f32[4,128,128]{2,1,0:T(8,128)} %add.39), channel_id=1, source_target_pairs={{0,8},{8,16},{16,24},{24,32},{32,40},{40,48},{48,56},{56,64},{64,7... | collective-permute-start | bytes 786440 | tf_op jit(solution)/shard_map/while/body/eval_jaxpr/ppermute | solution.py:21
  401.6 12.5 %collective-permute-start = (f32[4,128,128]{2,1,0:T(8,128)}, f32[4,128,128]{2,1,0:T(8,128)S(1)}, u32[]{:S(2)}, u32[]{:S(2)}) collective-permute-start(f32[4,128,128]{2,1,0:T(8,128)} %add.39), channel_id=1, source_target_pairs={{0,8},{8,16},{16,24},{24,32},{32,40},{40,48},{48,56},{56,64},{64,7... | collective-permute-start | bytes 786440 | tf_op jit(solution)/shard_map/while/body/eval_jaxpr/ppermute | solution.py:21
  415.8 11.8 %collective-permute-start = (f32[4,128,128]{2,1,0:T(8,128)}, f32[4,128,128]{2,1,0:T(8,128)S(1)}, u32[]{:S(2)}, u32[]{:S(2)}) collective-permute-start(f32[4,128,128]{2,1,0:T(8,128)} %add.39), channel_id=1, source_target_pairs={{0,8},{8,16},{16,24},{24,32},{32,40},{40,48},{48,56},{56,64},{64,7... | collective-permute-start | bytes 786440 | tf_op jit(solution)/shard_map/while/body/eval_jaxpr/ppermute | solution.py:21
  429.2 11.8 %collective-permute-start = (f32[4,128,128]{2,1,0:T(8,128)}, f32[4,128,128]{2,1,0:T(8,128)S(1)}, u32[]{:S(2)}, u32[]{:S(2)}) collective-permute-start(f32[4,128,128]{2,1,0:T(8,128)} %add.39), channel_id=1, source_target_pairs={{0,8},{8,16},{16,24},{24,32},{32,40},{40,48},{48,56},{56,64},{64,7... | collective-permute-start | bytes 786440 | tf_op jit(solution)/shard_map/while/body/eval_jaxpr/ppermute | solution.py:21
  442.7 11.8 %collective-permute-start = (f32[4,128,128]{2,1,0:T(8,128)}, f32[4,128,128]{2,1,0:T(8,128)S(1)}, u32[]{:S(2)}, u32[]{:S(2)}) collective-permute-start(f32[4,128,128]{2,1,0:T(8,128)} %add.39), channel_id=1, source_target_pairs={{0,8},{8,16},{16,24},{24,32},{32,40},{40,48},{48,56},{56,64},{64,7... | collective-permute-start | bytes 786440 | tf_op jit(solution)/shard_map/while/body/eval_jaxpr/ppermute | solution.py:21
  456.1 11.8 %collective-permute-start = (f32[4,128,128]{2,1,0:T(8,128)}, f32[4,128,128]{2,1,0:T(8,128)S(1)}, u32[]{:S(2)}, u32[]{:S(2)}) collective-permute-start(f32[4,128,128]{2,1,0:T(8,128)} %add.39), channel_id=1, source_target_pairs={{0,8},{8,16},{16,24},{24,32},{32,40},{40,48},{48,56},{56,64},{64,7... | collective-permute-start | bytes 786440 | tf_op jit(solution)/shard_map/while/body/eval_jaxpr/ppermute | solution.py:21
  469.6 11.8 %collective-permute-start = (f32[4,128,128]{2,1,0:T(8,128)}, f32[4,128,128]{2,1,0:T(8,128)S(1)}, u32[]{:S(2)}, u32[]{:S(2)}) collective-permute-start(f32[4,128,128]{2,1,0:T(8,128)} %add.39), channel_id=1, source_target_pairs={{0,8},{8,16},{16,24},{24,32},{32,40},{40,48},{48,56},{56,64},{64,7... | collective-permute-start | bytes 786440 | tf_op jit(solution)/shard_map/while/body/eval_jaxpr/ppermute | solution.py:21
  483.0 11.8 %collective-permute-start = (f32[4,128,128]{2,1,0:T(8,128)}, f32[4,128,128]{2,1,0:T(8,128)S(1)}, u32[]{:S(2)}, u32[]{:S(2)}) collective-permute-start(f32[4,128,128]{2,1,0:T(8,128)} %add.39), channel_id=1, source_target_pairs={{0,8},{8,16},{16,24},{24,32},{32,40},{40,48},{48,56},{56,64},{64,7... | collective-permute-start | bytes 786440 | tf_op jit(solution)/shard_map/while/body/eval_jaxpr/ppermute | solution.py:21
  497.5 4.2 copy-start.2
